TPU v7x, 512 devices: a whole 4x8x8 slice. The times are simulated.
512 devices in a mesh: rev: 8 (over z_lo, x), bin: 64 (over y, z_hi, core).
Axes of the slice: x: 4, y: 8, z: 8 (z_hi: 4, z_lo: 2; z = z_hi * 2 + z_lo), core: 2. Of those that a mesh axis runs over, the one named last changes fastest.
Arguments:
- snapshots: float32 [8, 512, 3, 24, 8, 128], P('rev', 'bin'), may hold values from -6 to 6
- phase_index: int32 [8, 512], P('rev', 'bin'), may hold values from 0 to 255, as said below
Outputs:
- stress_terms: float32 [4, 6, 256, 24, 8, 128], P(None, None, 'bin', 'rev')
- mean_velocity: float32 [3, 256, 24, 8, 128], P(None, 'bin', 'rev')
Inputs may be any that keep to these rules, and one draw needn't show every extreme that they name: `phase_index`: the rows b * 8 to (b + 1) * 8 - 1 of a revolution shard name bins b * 4 to (b + 1) * 4 - 1 only, and each of these bins at least once.
All inputs are finite; a program needn't handle non-finite values.
Results may differ from a plain program's by a relative error of at most 0.00017.
Values sent between devices are 32-bit elements; how exact they have to be, the bound alone decides.
No kernel may reach another device: no remote copies, remote signals or barrier semaphores. Data moves between devices by JAX's collectives and lax.ppermute only.
A program may use at most 64 MiB of HBM per device.

v0:
```python
import jax
import jax.numpy as jnp
from jax import lax
from jax.sharding import PartitionSpec as P

PHASES = 256
viscosity = 0.2
stress_pairs = ((0, 0), (0, 1), (0, 2), (1, 1), (1, 2), (2, 2))


def padded_2(cells, sides, width):
    for axis, dim in sides:
        count = lax.axis_size(axis)
        head = lax.slice_in_dim(cells, 0, width, axis=dim)
        tail = lax.slice_in_dim(cells, cells.shape[dim] - width, cells.shape[dim], axis=dim)
        cells = jnp.concatenate(
            [
                lax.ppermute(tail, axis, [(i, (i + 1) % count) for i in range(count)]),
                cells,
                lax.ppermute(head, axis, [((i + 1) % count, i) for i in range(count)]),
            ],
            axis=dim,
        )
    return cells


def pair_index(first, second):
    low, high = (min(first, second), max(first, second))
    return stress_pairs.index((low, high))


def binned(frames, weights):
    vel_x, vel_y, vel_z = (frames[:, 0], frames[:, 1], frames[:, 2])
    stacked = jnp.stack(
        [
            jnp.ones_like(vel_x),
            vel_x,
            vel_y,
            vel_z,
            vel_x * vel_x,
            vel_x * vel_y,
            vel_x * vel_z,
            vel_y * vel_y,
            vel_y * vel_z,
            vel_z * vel_z,
        ],
        axis=1,
    )
    return jnp.einsum("ps,sfxyz->xfpyz", weights, stacked, precision=lax.Precision.HIGHEST)


def first_diff(shifted):
    return (
        0.75 * (shifted(1) - shifted(-1))
        - 0.15 * (shifted(2) - shifted(-2))
        + (shifted(3) - shifted(-3)) / 60.0
    )


def second_diff(shifted, centre):
    return (
        -49.0 / 18.0 * centre
        + 1.5 * (shifted(1) + shifted(-1))
        - 0.15 * (shifted(2) + shifted(-2))
        + (shifted(3) + shifted(-3)) / 90.0
    )


def finish_terms(owned):
    planes, bins_dev = (owned.shape[0], owned.shape[2])
    samples = owned[:, 0]
    velocity = [owned[:, 1 + comp] / samples for comp in range(3)]
    stresses = [
        owned[:, 4 + slot] / samples - velocity[pair[0]] * velocity[pair[1]]
        for slot, pair in enumerate(stress_pairs)
    ]
    fields = jnp.stack(velocity + stresses, axis=1)
    padded = padded_2(fields, (("rev", 0), ("bin", 2)), 3)

    def along(component, dim, centre):
        source = padded[:, component]
        if dim == 0:
            return lambda amount: source[3 + amount : 3 + amount + planes, 3 : 3 + bins_dev]
        if dim == 3:
            return lambda amount: source[3 : 3 + planes, 3 + amount : 3 + amount + bins_dev]
        return lambda amount: jnp.roll(centre, -amount, dim + 1)

    grad_u = [
        [first_diff(along(comp, dim, velocity[comp])) for dim in range(3)] for comp in range(3)
    ]
    unsteady, convect, produce, diffuse = ([], [], [], [])
    for slot, pair in enumerate(stress_pairs):
        first, second = pair
        stress = stresses[slot]
        unsteady.append(first_diff(along(3 + slot, 3, stress)))
        grads = [first_diff(along(3 + slot, dim, stress)) for dim in range(3)]
        convect.append(velocity[0] * grads[0] + velocity[1] * grads[1] + velocity[2] * grads[2])
        summed = jnp.zeros_like(stress)
        for dim in range(3):
            summed = (
                summed
                + stresses[pair_index(first, dim)] * grad_u[second][dim]
                + stresses[pair_index(second, dim)] * grad_u[first][dim]
            )
        produce.append(-summed)
        diffuse.append(
            viscosity
            * (
                second_diff(along(3 + slot, 0, stress), stress)
                + second_diff(along(3 + slot, 1, stress), stress)
                + second_diff(along(3 + slot, 2, stress), stress)
            )
        )
    terms_all = jnp.stack(
        [jnp.stack(unsteady), jnp.stack(convect), jnp.stack(produce), jnp.stack(diffuse)]
    )
    return (
        jnp.transpose(terms_all, (0, 1, 3, 2, 4, 5)),
        jnp.transpose(jnp.stack(velocity), (0, 2, 1, 3, 4)),
    )


def shards(snapshots, phase_index):
    frames = snapshots[0]
    bins_dev = PHASES // lax.axis_size("bin")
    planes = frames.shape[2] // lax.axis_size("rev")
    local_bins = phase_index[0] - lax.axis_index("bin") * bins_dev
    one_hot = (local_bins[None, :] == jnp.arange(bins_dev, dtype=jnp.int32)[:, None]).astype(
        jnp.float32
    )
    summed = lax.psum(binned(frames, one_hot), "rev")
    owned = lax.dynamic_slice_in_dim(summed, lax.axis_index("rev") * planes, planes, 0)
    return finish_terms(owned)


def solution(mesh):
    in_specs = (P("rev", "bin", None, None, None, None), P("rev", "bin"))
    out_specs = (P(None, None, "bin", "rev", None, None), P(None, "bin", "rev", None, None))
    return jax.shard_map(shards, mesh=mesh, in_specs=in_specs, out_specs=out_specs, check_vma=False)
```

profile of v0, /device:TPU:31, one launch (start us, length us, event | category | flops | bytes accessed | tf_op | source)
XLA Modules:
  0.0 230.9 jit_solution(12959993338759327280)
XLA Ops:
  7.2 1.0 broadcast_dynamic-update-slice_fusion
  8.2 3.0 %copy.18 = f32[1,8,3,24,8,128]{5,1,4,3,2,0:T(8,128)S(1)} copy(f32[1,8,3,24,8,128]{5,4,3,2,1,0:T(8,128)} %param.2) | data formatting | bytes 4718592 | tf_op args[0]
  11.2 2.8 %constant_dynamic-update-slice_fusion = f32[8,10,24,8,128]{4,0,3,2,1:T(8,128)} fusion(f32[8,10,24,8,128]{4,0,3,2,1:T(8,128)} %broadcast_dynamic-update-slice_fusion, f32[1,8,3,24,8,128]{5,4,3,2,1,0:T(8,128)S(1)} %copy-done), kind=kLoop, calls=%fused_computation.22 | loop fusion | bytes 4718592
  14.0 0.9 multiply_dynamic-update-slice_fusion.5
  15.0 1.0 multiply_dynamic-update-slice_fusion.4
  16.0 1.0 multiply_dynamic-update-slice_fusion.3
  17.0 0.9 multiply_dynamic-update-slice_fusion.2
  17.9 1.0 multiply_dynamic-update-slice_fusion.1
  18.9 1.0 multiply_dynamic-update-slice_fusion
  20.0 9.0 %convolution_bitcast_fusion = f32[24,10,4,8,128]{4,2,3,0,1:T(4,128)} fusion(f32[8,10,24,8,128]{4,0,3,2,1:T(8,128)} %multiply_dynamic-update-slice_fusion, s32[8]{0:T(128)S(1)} %subtract_bitcast_fusion), kind=kOutput, calls=%fused_computation.2 | convolution fusion | flops 94371872 | bytes 11796512 | tf_op jit(solution)/shard_map/ps,sfxyz->xfpyz/dot_general | solution.py:49
  29.0 113.4 %all-reduce.2.cloned.1.call-done = f32[24,10,4,8,128]{4,2,3,0,1:T(4,128)} async-done(((f32[24,10,4,8,128]{4,2,3,0,1:T(4,128)}), f32[24,10,4,8,128]{4,2,3,0,1:T(4,128)}) %all-reduce.2.cloned.1.call-update) | async-done | bytes 3932176 | tf_op jit(solution)/shard_map/psum | solution.py:131
  142.4 0.8 constant_dynamic-update-slice_fusion.9
  143.2 0.9 constant_dynamic-update-slice_fusion.8
  144.1 0.9 constant_dynamic-update-slice_fusion.7
  144.9 0.9 constant_dynamic-update-slice_fusion.6
  145.8 0.9 constant_dynamic-update-slice_fusion.5
  146.7 0.9 constant_dynamic-update-slice_fusion.4
  147.5 0.9 constant_dynamic-update-slice_fusion.3
  148.4 0.9 constant_dynamic-update-slice_fusion.2
  149.2 0.9 constant_dynamic-update-slice_fusion.1
  150.1 4.4 %collective-permute-start = (f32[3,9,4,8,128]{4,2,3,0,1:T(4,128)S(1)}, f32[3,9,4,8,128]{4,2,3,0,1:T(4,128)S(1)}, u32[]{:S(2)}, u32[]{:S(2)}) collective-permute-start(f32[3,9,4,8,128]{4,2,3,0,1:T(4,128)S(1)} %constant_dynamic-update-slice_fusion.1), channel_id=1, source_target_pairs={{0,64},{64,128},{128,192},{192,256},{256,320},{320,384},{384,448},... | collective-permute-start | bytes 1327112 | tf_op jit(solution)/shard_map/ppermute | solution.py:18
  154.5 1.9 collective-permute-start.1
  158.0 5.1 %collective-permute-done = f32[3,9,4,8,128]{4,2,3,0,1:T(4,128)S(1)} collective-permute-done((f32[3,9,4,8,128]{4,2,3,0,1:T(4,128)S(1)}, f32[3,9,4,8,128]{4,2,3,0,1:T(4,128)S(1)}, u32[]{:S(2)}, u32[]{:S(2)}) %collective-permute-start) | collective-permute-done | bytes 442400 | tf_op jit(solution)/shard_map/ppermute | solution.py:18
  163.2 5.9 %collective-permute-done.1 = f32[3,9,4,8,128]{4,2,3,0,1:T(4,128)S(1)} collective-permute-done((f32[3,9,4,8,128]{4,2,3,0,1:T(4,128)S(1)}, f32[3,9,4,8,128]{4,2,3,0,1:T(4,128)S(1)}, u32[]{:S(2)}, u32[]{:S(2)}) %collective-permute-start.1) | collective-permute-done | bytes 442400 | tf_op jit(solution)/shard_map/ppermute | solution.py:20
  169.1 0.3 pad_maximum_fusion.1
  169.4 0.8 fusion.99
  170.3 6.2 %collective-permute-start.2 = (f32[9,9,3,8,128]{4,3,2,1,0:T(8,128)S(1)}, f32[9,9,3,8,128]{4,3,2,1,0:T(8,128)S(1)}, u32[]{:S(2)}, u32[]{:S(2)}) collective-permute-start(f32[9,9,3,8,128]{4,3,2,1,0:T(8,128)S(1)} %copy.8), channel_id=1, source_target_pairs={{0,1},{1,2},{2,3},{3,4},{4,5},{5,6},{6,7},{7,8},{8,9},{9,10},{10,1... | collective-permute-start | bytes 2985992 | tf_op jit(solution)/shard_map/ppermute | solution.py:18
  176.7 2.1 collective-permute-start.3
  178.8 0.7 copy.13
  179.9 15.0 %collective-permute-done.2 = f32[9,9,3,8,128]{4,3,2,1,0:T(8,128)S(1)} collective-permute-done((f32[9,9,3,8,128]{4,3,2,1,0:T(8,128)S(1)}, f32[9,9,3,8,128]{4,3,2,1,0:T(8,128)S(1)}, u32[]{:S(2)}, u32[]{:S(2)}) %collective-permute-start.2) | collective-permute-done | bytes 995360 | tf_op jit(solution)/shard_map/ppermute | solution.py:18
  194.9 0.4 copy.10
  195.3 13.2 %collective-permute-done.3 = f32[9,9,3,8,128]{4,3,2,1,0:T(8,128)S(1)} collective-permute-done((f32[9,9,3,8,128]{4,3,2,1,0:T(8,128)S(1)}, f32[9,9,3,8,128]{4,3,2,1,0:T(8,128)S(1)}, u32[]{:S(2)}, u32[]{:S(2)}) %collective-permute-start.3) | collective-permute-done | bytes 995360 | tf_op jit(solution)/shard_map/ppermute | solution.py:20
  208.4 0.4 copy.11
  208.8 1.6 pad_maximum_fusion
  210.4 0.7 slice_bitcast_fusion.3
  211.0 1.3 constant_dynamic-update-slice_fusion.27
  213.0 0.1 fusion.161
  213.1 0.1 fusion.160
  213.2 0.1 fusion.163
  213.3 0.1 fusion.162
  213.5 0.1 fusion.165
  213.6 0.1 fusion.164
  213.8 1.3 constant_dynamic-update-slice_fusion.26
  215.1 0.1 fusion.125
  215.2 0.1 fusion.124
  215.4 0.1 fusion.127
  215.5 0.1 fusion.126
  215.6 0.1 fusion.129
  215.7 0.1 fusion.128
  216.0 1.2 constant_dynamic-update-slice_fusion.25
  218.0 0.3 constant_dynamic-update-slice_fusion.21
  218.3 0.3 constant_dynamic-update-slice_fusion.33
  218.9 0.3 constant_dynamic-update-slice_fusion.20
  219.2 0.3 constant_dynamic-update-slice_fusion.32
  219.6 0.3 constant_dynamic-update-slice_fusion.19
  219.9 0.3 constant_dynamic-update-slice_fusion.31
  220.3 0.3 constant_dynamic-update-slice_fusion.18
  220.7 0.3 constant_dynamic-update-slice_fusion.30
  221.1 0.3 constant_dynamic-update-slice_fusion.17
  221.4 0.3 constant_dynamic-update-slice_fusion.29
  221.8 0.3 constant_dynamic-update-slice_fusion.16
  222.2 0.3 constant_dynamic-update-slice_fusion.28
  222.5 0.4 maximum_bitcast_fusion
  222.9 1.1 copy.12
  (91 shorter events, 4.0 us)
Async XLA Ops:
  7.2 4.1 %copy-start = (f32[1,8,3,24,8,128]{5,4,3,2,1,0:T(8,128)S(1)}, f32[1,8,3,24,8,128]{5,4,3,2,1,0:T(8,128)}, u32[]{:S(2)}) copy-start(f32[1,8,3,24,8,128]{5,4,3,2,1,0:T(8,128)} %param.2) | copy-start | bytes 7077892
  7.2 135.2 %all-reduce.2.cloned.1.call-start = ((), (), s32[]{:S(2)}) async-start(), calls=%async_computation | async-start | bytes 7864320 | tf_op jit(solution)/shard_map/psum | solution.py:131
  16.0 4.0 %copy-start.1 = (s32[1,8]{1,0:T(1,128)S(1)}, s32[1,8]{1,0:T(1,128)}, u32[]{:S(2)}) copy-start(s32[1,8]{1,0:T(1,128)} %param.3) | copy-start | bytes 100
  150.1 13.1 %collective-permute-start = (f32[3,9,4,8,128]{4,2,3,0,1:T(4,128)S(1)}, f32[3,9,4,8,128]{4,2,3,0,1:T(4,128)S(1)}, u32[]{:S(2)}, u32[]{:S(2)}) collective-permute-start(f32[3,9,4,8,128]{4,2,3,0,1:T(4,128)S(1)} %constant_dynamic-update-slice_fusion.1), channel_id=1, source_target_pairs={{0,64},{64,128},{128,192},{192,256},{256,320},{320,384},{384,448},... | collective-permute-start | bytes 1327112 | tf_op jit(solution)/shard_map/ppermute | solution.py:18
  154.5 14.6 %collective-permute-start.1 = (f32[3,9,4,8,128]{4,2,3,0,1:T(4,128)S(1)}, f32[3,9,4,8,128]{4,2,3,0,1:T(4,128)S(1)}, u32[]{:S(2)}, u32[]{:S(2)}) collective-permute-start(f32[3,9,4,8,128]{4,2,3,0,1:T(4,128)S(1)} %constant_dynamic-update-slice_fusion.1), channel_id=1, source_target_pairs={{64,0},{128,64},{192,128},{256,192},{320,256},{384,320},{448,384},... | collective-permute-start | bytes 1327112 | tf_op jit(solution)/shard_map/ppermute | solution.py:20
  170.3 24.5 %collective-permute-start.2 = (f32[9,9,3,8,128]{4,3,2,1,0:T(8,128)S(1)}, f32[9,9,3,8,128]{4,3,2,1,0:T(8,128)S(1)}, u32[]{:S(2)}, u32[]{:S(2)}) collective-permute-start(f32[9,9,3,8,128]{4,3,2,1,0:T(8,128)S(1)} %copy.8), channel_id=1, source_target_pairs={{0,1},{1,2},{2,3},{3,4},{4,5},{5,6},{6,7},{7,8},{8,9},{9,10},{10,1... | collective-permute-start | bytes 2985992 | tf_op jit(solution)/shard_map/ppermute | solution.py:18
  176.7 31.8 %collective-permute-start.3 = (f32[9,9,3,8,128]{4,3,2,1,0:T(8,128)S(1)}, f32[9,9,3,8,128]{4,3,2,1,0:T(8,128)S(1)}, u32[]{:S(2)}, u32[]{:S(2)}) collective-permute-start(f32[9,9,3,8,128]{4,3,2,1,0:T(8,128)S(1)} %copy.9), channel_id=1, source_target_pairs={{1,0},{2,1},{3,2},{4,3},{5,4},{6,5},{7,6},{8,7},{9,8},{10,9},{11,1... | collective-permute-start | bytes 2985992 | tf_op jit(solution)/shard_map/ppermute | solution.py:20
Sparse Core Ops, SparseCore 0:
  29.1 113.1 all-reduce.1
where the time goes:
time: 232 us; the launch traced here: 231 us
  waiting for transfers between devices  153 us (66%)
  other arithmetic  24.4 us (11%)
  local copies, waits for them, and re-layouts  15.3 us (7%)
  between operations  14.8 us (6%)
  starting transfers between devices  14.7 us (6%)
  matrix products  9 us (4%)
    psum x1, waiting for transfers between devices, shards(): summed = lax.psum(binned(frames, one_hot), 'rev')  113 us
    ppermute x2, waiting for transfers between devices, padded_2(): lax.ppermute(tail, axis, [(i, (i + 1) % count) for i in range(count)])  20.1 us
    unnamed x33, other arithmetic  19.4 us
    ppermute x2, waiting for transfers between devices, padded_2(): lax.ppermute(head, axis, [((i + 1) % count, i) for i in range(count)])  19.1 us
    ppermute x2, starting transfers between devices, padded_2(): lax.ppermute(tail, axis, [(i, (i + 1) % count) for i in range(count)])  10.6 us
    dot_general x1, matrix products, binned(): jnp.einsum('ps,sfxyz->xfpyz', weights, stacked, precision=lax.Precision.H...  9 us
    unnamed x9, local copies, waits for them, and re-layouts  8.58 us
  transfers between devices with their start and end apart: 5, of which 5 were waited for; matrix products, arithmetic and copies ran while one was open for 1% of the time, Pallas kernels for 0%

commit v1 on v0

--- a/solution.py
+++ b/solution.py
@@ -128,7 +128,7 @@
     one_hot = (local_bins[None, :] == jnp.arange(bins_dev, dtype=jnp.int32)[:, None]).astype(
         jnp.float32
     )
-    summed = lax.psum(binned(frames, one_hot), "rev")
+    summed = jnp.sum(lax.all_gather(binned(frames, one_hot), "rev"), axis=0)
     owned = lax.dynamic_slice_in_dim(summed, lax.axis_index("rev") * planes, planes, 0)
     return finish_terms(owned)
 

time: 232 us -> 448 us (1.93)
  waiting for transfers between devices: 153 us -> 355 us
  other arithmetic: 24.4 us -> 38.2 us
    all_gather x0 -> x1, waiting for transfers between devices: none -> 316 us  [shards(): summed = jnp.sum(lax.all_gather(binned(frames, one_hot), 'rev'), axis=0)]
    psum x1 -> x0, waiting for transfers between devices: 113 us -> none  [shards(): summed = lax.psum(binned(frames, one_hot), 'rev')]
    reduce_sum x0 -> x1, other arithmetic: none -> 13.8 us  [shards(): summed = jnp.sum(lax.all_gather(binned(frames, one_hot), 'rev'), axis=0)]
where the time goes in v1:
time: 448 us; the launch traced here: 447 us
  waiting for transfers between devices  355 us (79%)
  other arithmetic  38.2 us (9%)
  local copies, waits for them, and re-layouts  15.3 us (3%)
  between operations  14.8 us (3%)
  starting transfers between devices  14.4 us (3%)
  matrix products  8.88 us (2%)
    all_gather x1, waiting for transfers between devices, shards(): summed = jnp.sum(lax.all_gather(binned(frames, one_hot), 'rev'), axis=0)  316 us
    ppermute x2, waiting for transfers between devices, padded_2(): lax.ppermute(tail, axis, [(i, (i + 1) % count) for i in range(count)])  20.1 us
    unnamed x33, other arithmetic  19.4 us
    ppermute x2, waiting for transfers between devices, padded_2(): lax.ppermute(head, axis, [((i + 1) % count, i) for i in range(count)])  19.3 us
    reduce_sum x1, other arithmetic, shards(): summed = jnp.sum(lax.all_gather(binned(frames, one_hot), 'rev'), axis=0)  13.8 us
    ppermute x2, starting transfers between devices, padded_2(): lax.ppermute(tail, axis, [(i, (i + 1) % count) for i in range(count)])  10.6 us
  transfers between devices with their start and end apart: 5, of which 5 were waited for; matrix products, arithmetic and copies ran while one was open for 1% of the time, Pallas kernels for 0%

profile of v1, /device:TPU:31, one launch (start us, length us, event | category | flops | bytes accessed | tf_op | source)
XLA Modules:
  0.0 446.9 jit_solution(11801526400986275288)
XLA Ops:
  7.2 1.0 broadcast_dynamic-update-slice_fusion
  8.2 3.0 copy.19
  11.2 2.8 constant_dynamic-update-slice_fusion
  14.0 0.9 multiply_dynamic-update-slice_fusion.5
  15.0 1.0 multiply_dynamic-update-slice_fusion.4
  16.0 1.0 multiply_dynamic-update-slice_fusion.3
  17.0 0.9 multiply_dynamic-update-slice_fusion.2
  17.9 1.0 multiply_dynamic-update-slice_fusion.1
  18.9 1.0 multiply_dynamic-update-slice_fusion
  20.0 8.9 %convolution_bitcast_fusion = f32[24,10,4,8,128]{4,2,3,0,1:T(4,128)} fusion(f32[8,10,24,8,128]{4,0,3,2,1:T(8,128)} %multiply_dynamic-update-slice_fusion, s32[8]{0:T(128)S(1)} %subtract_bitcast_fusion), kind=kOutput, calls=%fused_computation.2 | convolution fusion | flops 94371872 | bytes 11796512 | tf_op jit(solution)/shard_map/ps,sfxyz->xfpyz/dot_general | solution.py:49
  28.9 315.7 %all-gather.3.cloned.1.call-done = f32[192,10,4,8,128]{4,2,3,0,1:T(4,128)} async-done(((f32[24,10,4,8,128]{4,2,3,0,1:T(4,128)}), f32[192,10,4,8,128]{4,2,3,0,1:T(4,128)}) %all-gather.3.cloned.1.call-update) | async-done | bytes 31457296 | tf_op jit(solution)/shard_map/all_gather | solution.py:131
  344.6 13.8 %reduce_sum.9 = f32[24,10,4,8,128]{4,2,3,0,1:T(4,128)} reduce(f32[8,24,10,4,8,128]{5,3,4,1,0,2:T(4,128)} %bitcast.213, f32[]{:T(128)} %constant.73.clone.1), dimensions={0}, to_apply=%region_0.0 | reduce | flops 6881280 | bytes 35389444 | tf_op jit(solution)/shard_map/reduce_sum | solution.py:131
  358.5 0.8 constant_dynamic-update-slice_fusion.9
  359.3 0.9 constant_dynamic-update-slice_fusion.8
  360.2 0.9 constant_dynamic-update-slice_fusion.7
  361.0 0.9 constant_dynamic-update-slice_fusion.6
  361.9 0.9 constant_dynamic-update-slice_fusion.5
  362.8 0.9 constant_dynamic-update-slice_fusion.4
  363.6 0.9 constant_dynamic-update-slice_fusion.3
  364.5 0.9 constant_dynamic-update-slice_fusion.2
  365.3 0.9 constant_dynamic-update-slice_fusion.1
  366.2 4.2 collective-permute-start
  370.4 1.9 collective-permute-start.1
  373.9 5.1 %collective-permute-done = f32[3,9,4,8,128]{4,2,3,0,1:T(4,128)S(1)} collective-permute-done((f32[3,9,4,8,128]{4,2,3,0,1:T(4,128)S(1)}, f32[3,9,4,8,128]{4,2,3,0,1:T(4,128)S(1)}, u32[]{:S(2)}, u32[]{:S(2)}) %collective-permute-start) | collective-permute-done | bytes 442400 | tf_op jit(solution)/shard_map/ppermute | solution.py:18
  379.0 5.9 %collective-permute-done.1 = f32[3,9,4,8,128]{4,2,3,0,1:T(4,128)S(1)} collective-permute-done((f32[3,9,4,8,128]{4,2,3,0,1:T(4,128)S(1)}, f32[3,9,4,8,128]{4,2,3,0,1:T(4,128)S(1)}, u32[]{:S(2)}, u32[]{:S(2)}) %collective-permute-start.1) | collective-permute-done | bytes 442400 | tf_op jit(solution)/shard_map/ppermute | solution.py:20
  385.0 0.3 pad_maximum_fusion.1
  385.3 0.8 fusion.99
  386.2 6.4 %collective-permute-start.2 = (f32[9,9,3,8,128]{4,3,2,1,0:T(8,128)S(1)}, f32[9,9,3,8,128]{4,3,2,1,0:T(8,128)S(1)}, u32[]{:S(2)}, u32[]{:S(2)}) collective-permute-start(f32[9,9,3,8,128]{4,3,2,1,0:T(8,128)S(1)} %copy.9), channel_id=1, source_target_pairs={{0,1},{1,2},{2,3},{3,4},{4,5},{5,6},{6,7},{7,8},{8,9},{9,10},{10,1... | collective-permute-start | bytes 2985992 | tf_op jit(solution)/shard_map/ppermute | solution.py:18
  392.7 1.9 collective-permute-start.3
  394.7 0.7 copy.14
  395.8 15.0 %collective-permute-done.2 = f32[9,9,3,8,128]{4,3,2,1,0:T(8,128)S(1)} collective-permute-done((f32[9,9,3,8,128]{4,3,2,1,0:T(8,128)S(1)}, f32[9,9,3,8,128]{4,3,2,1,0:T(8,128)S(1)}, u32[]{:S(2)}, u32[]{:S(2)}) %collective-permute-start.2) | collective-permute-done | bytes 995360 | tf_op jit(solution)/shard_map/ppermute | solution.py:18
  410.8 0.4 copy.11
  411.1 13.4 %collective-permute-done.3 = f32[9,9,3,8,128]{4,3,2,1,0:T(8,128)S(1)} collective-permute-done((f32[9,9,3,8,128]{4,3,2,1,0:T(8,128)S(1)}, f32[9,9,3,8,128]{4,3,2,1,0:T(8,128)S(1)}, u32[]{:S(2)}, u32[]{:S(2)}) %collective-permute-start.3) | collective-permute-done | bytes 995360 | tf_op jit(solution)/shard_map/ppermute | solution.py:20
  424.5 0.4 copy.12
  424.9 1.6 pad_maximum_fusion
  426.5 0.7 slice_bitcast_fusion.3
  427.1 1.3 constant_dynamic-update-slice_fusion.27
  429.0 0.1 fusion.161
  429.2 0.1 fusion.160
  429.3 0.1 fusion.163
  429.4 0.1 fusion.162
  429.5 0.1 fusion.165
  429.7 0.1 fusion.164
  429.9 1.3 constant_dynamic-update-slice_fusion.26
  431.3 0.1 fusion.124
  431.4 0.1 fusion.127
  431.6 0.1 fusion.126
  431.7 0.1 fusion.129
  431.8 0.1 fusion.128
  432.1 1.2 constant_dynamic-update-slice_fusion.25
  434.0 0.3 constant_dynamic-update-slice_fusion.21
  434.3 0.3 constant_dynamic-update-slice_fusion.33
  434.9 0.3 constant_dynamic-update-slice_fusion.20
  435.3 0.3 constant_dynamic-update-slice_fusion.32
  435.7 0.3 constant_dynamic-update-slice_fusion.19
  436.0 0.3 constant_dynamic-update-slice_fusion.31
  436.4 0.3 constant_dynamic-update-slice_fusion.18
  436.8 0.3 constant_dynamic-update-slice_fusion.30
  437.2 0.3 constant_dynamic-update-slice_fusion.17
  437.5 0.3 constant_dynamic-update-slice_fusion.29
  437.9 0.3 constant_dynamic-update-slice_fusion.16
  438.2 0.3 constant_dynamic-update-slice_fusion.28
  438.6 0.4 maximum_bitcast_fusion
  439.0 1.1 copy.13
  (92 shorter events, 4.1 us)
Async XLA Ops:
  7.2 4.1 copy-start
  7.2 337.5 %all-gather.3.cloned.1.call-start = ((), (), s32[]{:S(2)}) async-start(), calls=%async_computation | async-start | bytes 35389440 | tf_op jit(solution)/shard_map/all_gather | solution.py:131
  16.0 4.0 copy-start.1
  366.2 12.8 %collective-permute-start = (f32[3,9,4,8,128]{4,2,3,0,1:T(4,128)S(1)}, f32[3,9,4,8,128]{4,2,3,0,1:T(4,128)S(1)}, u32[]{:S(2)}, u32[]{:S(2)}) collective-permute-start(f32[3,9,4,8,128]{4,2,3,0,1:T(4,128)S(1)} %constant_dynamic-update-slice_fusion.1), channel_id=1, source_target_pairs={{0,64},{64,128},{128,192},{192,256},{256,320},{320,384},{384,448},... | collective-permute-start | bytes 1327112 | tf_op jit(solution)/shard_map/ppermute | solution.py:18
  370.4 14.6 %collective-permute-start.1 = (f32[3,9,4,8,128]{4,2,3,0,1:T(4,128)S(1)}, f32[3,9,4,8,128]{4,2,3,0,1:T(4,128)S(1)}, u32[]{:S(2)}, u32[]{:S(2)}) collective-permute-start(f32[3,9,4,8,128]{4,2,3,0,1:T(4,128)S(1)} %constant_dynamic-update-slice_fusion.1), channel_id=1, source_target_pairs={{64,0},{128,64},{192,128},{256,192},{320,256},{384,320},{448,384},... | collective-permute-start | bytes 1327112 | tf_op jit(solution)/shard_map/ppermute | solution.py:20
  386.2 24.5 %collective-permute-start.2 = (f32[9,9,3,8,128]{4,3,2,1,0:T(8,128)S(1)}, f32[9,9,3,8,128]{4,3,2,1,0:T(8,128)S(1)}, u32[]{:S(2)}, u32[]{:S(2)}) collective-permute-start(f32[9,9,3,8,128]{4,3,2,1,0:T(8,128)S(1)} %copy.9), channel_id=1, source_target_pairs={{0,1},{1,2},{2,3},{3,4},{4,5},{5,6},{6,7},{7,8},{8,9},{9,10},{10,1... | collective-permute-start | bytes 2985992 | tf_op jit(solution)/shard_map/ppermute | solution.py:18
  392.7 31.8 %collective-permute-start.3 = (f32[9,9,3,8,128]{4,3,2,1,0:T(8,128)S(1)}, f32[9,9,3,8,128]{4,3,2,1,0:T(8,128)S(1)}, u32[]{:S(2)}, u32[]{:S(2)}) collective-permute-start(f32[9,9,3,8,128]{4,3,2,1,0:T(8,128)S(1)} %copy.10), channel_id=1, source_target_pairs={{1,0},{2,1},{3,2},{4,3},{5,4},{6,5},{7,6},{8,7},{9,8},{10,9},{11,1... | collective-permute-start | bytes 2985992 | tf_op jit(solution)/shard_map/ppermute | solution.py:20
Sparse Core Ops, SparseCore 0:
  29.0 315.5 all-gather.2
